TPU v7x, 128 devices: a whole 4x4x4 slice. The times are simulated.
128 devices in a mesh: prow: 8 (over x, core), pcol: 16 (over y, z).
Axes of the slice: x: 4, y: 4, z: 4, core: 2. Of those that a mesh axis runs over, the one named last changes fastest.
Arguments:
- basis: bfloat16 [512, 256], replicated, may hold values from -0.25 to 0.25
- potentials: float32 [8, 512], replicated, may hold values from -6 to 6
- orbitals: bfloat16 [64, 512], P('pcol'), may hold values from -6 to 6
- chan_orbital: int32 [256], replicated, may hold values from 0 to 63
- pair_list: int32 [24576, 3], P(('prow', 'pcol')), may hold values from 0 to 255, as said below
- slot_list: int32 [24576], P(('prow', 'pcol')), may hold values from 0 to 255
- coefs: float32 [24576, 2], P(('prow', 'pcol')), may hold values from -6 to 6
- exchange_ops: bfloat16 [24576, 128, 256], P(('prow', 'pcol')), may hold values from -1.1953125 to 1.1953125
Outputs:
- hamiltonian: bfloat16 [32, 8, 2, 16, 256, 256], P(None, 'prow', None, 'pcol')
Inputs may be any that keep to these rules, and one draw needn't show every extreme that they name: `pair_list`: columns 0 and 1 are channels a, b; column 2 is a multipole order below 8. (b // 16 - a // 16) modulo 256 // 16 is below 2. Terms of one device with the same slot s have the same two channels, and the block (a, b) belongs to owner s // 2 in prow-major order: a % 8 and b % 16 are that owner's prow and pcol indices.
All inputs are finite; a program needn't handle non-finite values.
Results may differ from a plain program's by a relative error of at most 0.0058.
Values may be sent and summed in bfloat16 or wider, within the bound.
No kernel may reach another device: no remote copies, remote signals or barrier semaphores. Data moves between devices by JAX's collectives and lax.ppermute only.
A program may use at most 320 MiB of HBM per device.

v0:
```python
import jax
import jax.numpy as jnp
from jax import lax
from jax.sharding import PartitionSpec as P

CAP = 2
BAND = 2
RBLK = 32


def build_tiles(weights_group, exchange_group, basis):
    weights_group = lax.optimization_barrier(weights_group)
    scaled = (
        weights_group.astype(jnp.float32)[:, :, None] * basis.astype(jnp.float32)[None]
    ).astype(jnp.bfloat16)
    inner_rows = basis[: exchange_group.shape[1]]
    local_part = jnp.einsum("qa,gqb->gab", basis, scaled, preferred_element_type=jnp.float32)
    exchange_part = jnp.einsum(
        "qa,gqb->gab", inner_rows, exchange_group, preferred_element_type=jnp.float32
    )
    return (local_part + exchange_part).astype(jnp.bfloat16)


def sum_blocks(built_tiles, idents, block_count):
    select = (jnp.arange(block_count, dtype=jnp.int32)[:, None] == idents[None, :]).astype(
        jnp.bfloat16
    )
    spline_width = built_tiles.shape[1]
    summed = jnp.dot(
        select,
        built_tiles.reshape(built_tiles.shape[0], spline_width * spline_width),
        preferred_element_type=jnp.float32,
    )
    return summed.reshape(block_count, spline_width, spline_width)


def on_device(basis, potentials, orbitals, chan_orbital, pair_list, slot_list, coefs, exchange_ops):
    all_orbitals = lax.all_gather(orbitals, "pcol", axis=0, tiled=True)
    row_devs = lax.axis_size("prow")
    col_devs = lax.axis_size("pcol")
    slot_count = row_devs * col_devs * CAP
    chan_count = chan_orbital.shape[0]
    orb_count = all_orbitals.shape[0]
    point_count = basis.shape[0]
    spline_count = basis.shape[1]
    inner_count = exchange_ops.shape[1]
    term_count = exchange_ops.shape[0]
    col_groups = chan_count // col_devs
    block_count = RBLK * BAND
    first_chan = pair_list[:, 0]
    second_chan = pair_list[:, 1]
    multipole = pair_list[:, 2]
    channels = jnp.arange(chan_count, dtype=jnp.int32)
    orb_ids = jnp.arange(orb_count, dtype=jnp.int32)
    first_orb = jnp.sum(
        jnp.where(first_chan[:, None] == channels[None, :], chan_orbital[None, :], 0), axis=1
    )
    second_orb = jnp.sum(
        jnp.where(second_chan[:, None] == channels[None, :], chan_orbital[None, :], 0), axis=1
    )
    first_rows = jnp.dot(
        (first_orb[:, None] == orb_ids[None, :]).astype(jnp.bfloat16),
        all_orbitals,
        preferred_element_type=jnp.float32,
    )
    second_rows = jnp.dot(
        (second_orb[:, None] == orb_ids[None, :]).astype(jnp.bfloat16),
        all_orbitals,
        preferred_element_type=jnp.float32,
    )
    pick_pot = (
        multipole[:, None] == jnp.arange(potentials.shape[0], dtype=jnp.int32)[None, :]
    ).astype(jnp.float32)
    pot_rows = jnp.dot(pick_pot, potentials, precision=lax.Precision.HIGHEST)
    radial = coefs[:, 0:1] * pot_rows + coefs[:, 1:2] * (first_rows * second_rows)
    matches = slot_list[None, :] == jnp.arange(slot_count, dtype=jnp.int32)[:, None]
    slot_weight = jnp.dot(
        matches.astype(jnp.float32), radial, precision=lax.Precision.HIGHEST
    ).astype(jnp.bfloat16)
    exchange_rows = exchange_ops.reshape(term_count, inner_count * spline_count)
    slot_exchange = jnp.dot(
        matches.astype(jnp.bfloat16), exchange_rows, preferred_element_type=jnp.float32
    ).astype(jnp.bfloat16)
    slot_exchange = slot_exchange.reshape(slot_count, inner_count, spline_count)
    offset = jnp.mod(second_chan // col_devs - first_chan // col_devs, col_groups)
    block_index = first_chan // row_devs * BAND + offset
    slot_ids = jnp.max(jnp.where(matches, block_index[None, :], -1), axis=1)
    built_tiles = lax.map(
        lambda slot_group: build_tiles(slot_group[0], slot_group[1], basis),
        (
            slot_weight.reshape(slot_count // 16, 16, point_count),
            slot_exchange.reshape(slot_count // 16, 16, inner_count, spline_count),
        ),
    )
    built_tiles = built_tiles.reshape(row_devs, col_devs, CAP, spline_count, spline_count)
    received, idents = (
        lax.all_to_all(
            lax.all_to_all(built_tiles, "prow", split_axis=0, concat_axis=0, tiled=True),
            "pcol",
            split_axis=1,
            concat_axis=1,
            tiled=True,
        ),
        lax.all_to_all(
            lax.all_to_all(
                slot_ids.reshape(row_devs, col_devs, CAP),
                "prow",
                split_axis=0,
                concat_axis=0,
                tiled=True,
            ),
            "pcol",
            split_axis=1,
            concat_axis=1,
            tiled=True,
        ),
    )
    blocks = sum_blocks(
        received.reshape(slot_count, spline_count, spline_count),
        idents.reshape(slot_count),
        block_count,
    )
    return blocks.astype(jnp.bfloat16).reshape(RBLK, 1, BAND, 1, spline_count, spline_count)


def solution(mesh):
    placed = (
        P(),
        P(),
        P("pcol", None),
        P(),
        P(("prow", "pcol"), None),
        P(("prow", "pcol")),
        P(("prow", "pcol"), None),
        P(("prow", "pcol"), None, None),
    )
    return jax.shard_map(
        on_device,
        mesh=mesh,
        in_specs=placed,
        out_specs=P(None, "prow", None, "pcol", None, None),
        check_vma=False,
    )
```

profile of v0, /device:TPU:80, one launch (start us, length us, event | category | flops | bytes accessed | tf_op | source)
XLA Modules:
  0.0 1376.1 jit_solution(16522838021894493454)
XLA Ops:
  2.5 4.3 all-to-all-start
  8.5 21.0 %all-gather = bf16[16,4,512]{2,1,0:T(4,128)(2,1)S(1)} all-gather(bf16[1,4,512]{2,1,0:T(4,128)(2,1)} %bitcast.71), channel_id=1, replica_groups=mesh['prow'=8,'pcol'=16] {'pcol'}, dimensions={0}, use_global_device_ids=true | all-gather | bytes 69632 | tf_op jit(solution)/shard_map/all_gather | solution.py:38
  31.6 13.9 %copy.50 = bf16[24,8,128,256]{3,1,2,0:T(8,128)(2,1)} copy(bf16[24,8,128,256]{3,2,1,0:T(8,128)(2,1)} %bitcast.62) | data formatting | bytes 25165824
  45.5 12.7 convolution_convert_fusion
  58.2 15.7 %copy.51 = bf16[32,8,128,256]{3,2,1,0:T(8,128)(2,1)} copy(bf16[32,8,128,256]{3,1,2,0:T(8,128)(2,1)} %bitcast.58) | data formatting | bytes 33554432
  73.9 144.8 %while.10 = (s32[]{:T(128)}, bf16[16,16,256,256]{3,2,1,0:T(8,128)(2,1)}, bf16[16,16,512]{2,1,0:T(8,128)(2,1)S(1)}, bf16[512,256]{1,0:T(8,128)(2,1)S(1)}, bf16[16,16,128,256]{3,2,1,0:T(8,128)(2,1)}, /*index=5*/s32[]{:T(128)}) while((s32[]{:T(128)}, bf16[16,16,256,256]{3,2,1,0:T(8,128)(2,1)}, bf16[16,16,512]{2,1,0:T(8,128)(2,1)S(1)}, ...), condition=%wide.region_4.5_spmd, body=%wide.region_3.4_spmd.sunk | while | flops 1348476928 | bytes 21676120 | solution.py:88
  75.3 3.3 fusion.40
  78.6 2.8 copy.56
  81.5 1.5 constant_dynamic-update-slice_fusion.2
  84.4 3.3 fusion.40
  87.7 2.8 copy.56
  90.5 1.4 constant_dynamic-update-slice_fusion.2
  93.4 3.3 fusion.40
  96.7 2.8 copy.56
  99.6 1.5 constant_dynamic-update-slice_fusion.2
  102.5 3.3 fusion.40
  105.8 2.8 copy.56
  108.6 1.5 constant_dynamic-update-slice_fusion.2
  111.5 3.3 fusion.40
  114.8 2.8 copy.56
  117.7 1.5 constant_dynamic-update-slice_fusion.2
  120.6 3.3 fusion.40
  123.9 2.8 copy.56
  126.8 1.5 constant_dynamic-update-slice_fusion.2
  129.7 3.3 fusion.40
  133.0 2.8 copy.56
  135.8 1.5 constant_dynamic-update-slice_fusion.2
  138.7 3.3 fusion.40
  142.0 2.8 copy.56
  144.9 1.5 constant_dynamic-update-slice_fusion.2
  147.7 3.3 fusion.40
  151.0 2.8 copy.56
  153.9 1.5 constant_dynamic-update-slice_fusion.2
  156.8 3.3 fusion.40
  160.1 2.8 copy.56
  163.0 1.4 constant_dynamic-update-slice_fusion.2
  165.8 3.3 fusion.40
  169.1 2.8 copy.56
  172.0 1.5 constant_dynamic-update-slice_fusion.2
  174.9 3.3 fusion.40
  178.2 2.8 copy.56
  181.0 1.5 constant_dynamic-update-slice_fusion.2
  184.0 3.3 fusion.40
  187.3 2.8 copy.56
  190.1 1.5 constant_dynamic-update-slice_fusion.2
  193.0 3.3 fusion.40
  196.3 2.8 copy.56
  199.2 1.5 constant_dynamic-update-slice_fusion.2
  202.1 3.3 fusion.40
  205.4 2.8 copy.56
  208.2 1.5 constant_dynamic-update-slice_fusion.2
  211.1 3.3 fusion.40
  214.4 2.8 copy.56
  218.7 7.2 all-to-all-start.2
  226.6 363.6 %all-to-all-done.2 = bf16[8,16,2,256,256]{4,3,2,1,0:T(8,128)(2,1)} async-done(((bf16[8,16,2,256,256]{4,3,2,1,0:T(8,128)(2,1)}), bf16[8,16,2,256,256]{4,3,2,1,0:T(8,128)(2,1)}, u32[]{:S(2)}, u32[]{:S(2)}) %all-to-all-start.2) | async-done | bytes 33554464 | tf_op jit(solution)/shard_map/all_to_all | solution.py:98
  590.2 8.3 all-to-all-start.1
  598.5 23.0 %copy.42 = bf16[8,16,2,256,256]{4,3,2,0,1:T(8,128)(2,1)} copy(bf16[8,16,2,256,256]{4,3,2,1,0:T(8,128)(2,1)} %all-to-all-done.2) | data formatting | bytes 67108864 | tf_op jit(solution)/shard_map/all_to_all | solution.py:98
  621.4 7.2 all-to-all-start.3
  629.0 618.7 %all-to-all-done.3 = bf16[8,16,2,256,256]{4,3,2,0,1:T(8,128)(2,1)} async-done(((bf16[8,16,2,256,256]{4,3,2,0,1:T(8,128)(2,1)}), bf16[8,16,2,256,256]{4,3,2,0,1:T(8,128)(2,1)}, u32[]{:S(2)}, u32[]{:S(2)}) %all-to-all-start.3) | async-done | bytes 33554464 | tf_op jit(solution)/shard_map/all_to_all | solution.py:97
  1247.7 23.0 %copy.43 = bf16[8,16,2,256,256]{4,3,2,1,0:T(8,128)(2,1)} copy(bf16[8,16,2,256,256]{4,3,2,0,1:T(8,128)(2,1)} %all-to-all-done.3) | data formatting | bytes 67108864 | tf_op jit(solution)/shard_map/all_to_all | solution.py:97
  1270.7 31.0 %copy.52 = bf16[32,8,256,256]{3,1,2,0:T(8,128)(2,1)} copy(bf16[32,8,256,256]{3,2,1,0:T(8,128)(2,1)} %bitcast.56) | data formatting | bytes 67108864
  1301.7 44.0 %copy.44 = bf16[65536,256]{1,0:T(8,128)(2,1)} copy(bf16[65536,256]{0,1:T(8,128)(2,1)} %bitcast.57) | data formatting | bytes 67108864 | tf_op jit(solution)/shard_map/dot_general | solution.py:29
  1345.6 18.9 %convolution_convert_fusion.1 = bf16[64,256,256]{2,0,1:T(8,128)(2,1)} fusion(bf16[256,256,256]{2,1,0:T(8,128)(2,1)} %bitcast.55, s32[256]{0:T(256)S(1)} %eq.101), kind=kOutput, calls=%fused_computation.15 | convolution fusion | flops 2151694336 | bytes 41944064 | tf_op jit(solution)/shard_map/dot_general | solution.py:29
  1364.5 11.5 copy.46
  (91 shorter events, 31.2 us)
Async XLA Ops:
  0.0 30.0 %copy-start = (f32[8,512]{1,0:T(8,128)S(1)}, f32[8,512]{1,0:T(8,128)}, u32[]{:S(2)}) copy-start(f32[8,512]{1,0:T(8,128)} %param.11) | copy-start | bytes 49156
  0.0 45.5 %copy-start.3 = (s32[192]{0:T(256)S(1)}, s32[192]{0:T(256)}, u32[]{:S(2)}) copy-start(s32[192]{0:T(256)} %param.15) | copy-start | bytes 2308
  2.5 216.2 %all-to-all-start = ((s32[8,16,2]{1,2,0:T(2,128)}), s32[8,16,2]{1,2,0:T(2,128)S(1)}, u32[]{:S(2)}, u32[]{:S(2)}) async-start(s32[8,16,2]{1,2,0:T(2,128)} %copy.37), calls=%async_computation | async-start | bytes 16384 | tf_op jit(solution)/shard_map/all_to_all | solution.py:105
  58.2 15.7 %copy-start.2 = (bf16[512,256]{1,0:T(8,128)(2,1)S(1)}, bf16[512,256]{1,0:T(8,128)(2,1)}, u32[]{:S(2)}) copy-start(bf16[512,256]{1,0:T(8,128)(2,1)} %param.10) | copy-start | bytes 786436
  218.7 371.5 %all-to-all-start.2 = ((bf16[8,16,2,256,256]{4,3,2,1,0:T(8,128)(2,1)}), bf16[8,16,2,256,256]{4,3,2,1,0:T(8,128)(2,1)}, u32[]{:S(2)}, u32[]{:S(2)}) async-start(bf16[8,16,2,256,256]{4,3,2,1,0:T(8,128)(2,1)} %bitcast.60), calls=%async_computation.2 | async-start | bytes 67108864 | tf_op jit(solution)/shard_map/all_to_all | solution.py:98
  590.2 31.2 %all-to-all-start.1 = ((s32[8,16,2]{0,2,1:T(2,128)}), s32[8,16,2]{0,2,1:T(2,128)S(1)}, u32[]{:S(2)}, u32[]{:S(2)}) async-start(s32[8,16,2]{0,2,1:T(2,128)} %copy.38), calls=%async_computation.1 | async-start | bytes 32768 | tf_op jit(solution)/shard_map/all_to_all | solution.py:104
  621.4 626.3 %all-to-all-start.3 = ((bf16[8,16,2,256,256]{4,3,2,0,1:T(8,128)(2,1)}), bf16[8,16,2,256,256]{4,3,2,0,1:T(8,128)(2,1)}, u32[]{:S(2)}, u32[]{:S(2)}) async-start(bf16[8,16,2,256,256]{4,3,2,0,1:T(8,128)(2,1)} %copy.42), calls=%async_computation.3 | async-start | bytes 67108864 | tf_op jit(solution)/shard_map/all_to_all | solution.py:97
  1345.6 30.5 %copy-start.1 = (f32[8,512]{1,0:T(8,128)S(1)}, f32[8,512]{1,0:T(8,128)}, u32[]{:S(2)}) copy-start(f32[8,512]{1,0:T(8,128)} %param.11) | copy-start | bytes 49156
where the time goes:
time: 1380 us
  waiting for transfers between devices  982 us (71%)
  local copies, waits for them, and re-layouts  237 us (17%)
  matrix products  107 us (8%)
  starting transfers between devices  27 us (2%)
  blocking collectives  21 us (2%)
    all_to_all x1, waiting for transfers between devices, on_device(): lax.all_to_all(lax.all_to_all(built_tiles, 'prow', split_axis=0, concat_a...  619 us
    all_to_all x1, waiting for transfers between devices, on_device(): lax.all_to_all(built_tiles, 'prow', split_axis=0, concat_axis=0, tiled=True)  364 us
    dynamic_update_slice x32, local copies, waits for them, and re-layouts, on_device(): lax.map(lambda slot_group: build_tiles(slot_group[0], slot_group[1], basi...  69.1 us
    unnamed x12, local copies, waits for them, and re-layouts  60.6 us
    dot_general x16, matrix products, build_tiles(): jnp.einsum('qa,gqb->gab', inner_rows, exchange_group, preferred_element_t...  52.9 us
    dot_general x1, local copies, waits for them, and re-layouts, sum_blocks(): jnp.dot(select, built_tiles.reshape(built_tiles.shape[0], spline_width *...  44 us
  transfers between devices with their start and end apart: 4, of which 2 were waited for; matrix products, arithmetic and copies ran while one was open for 16% of the time, Pallas kernels for 0%

commit v1 on v0

--- a/solution.py
+++ b/solution.py
@@ -6,6 +6,22 @@
 CAP = 2
 BAND = 2
 RBLK = 32
+
+
+def pairwise_exchange(x, axis, split, join):
+    ways, here = (lax.axis_size(axis), lax.axis_index(axis))
+    width = x.shape[split] // ways
+    lengths = list(x.shape)
+    lengths[split] = width
+    height = lengths[join]
+    lengths[join] = height * ways
+    full = jnp.zeros(lengths, x.dtype)
+    for mask in range(ways):
+        part = lax.dynamic_slice_in_dim(x, (here ^ mask) * width, width, axis=split)
+        if mask:
+            part = lax.ppermute(part, axis, [(d, d ^ mask) for d in range(ways)])
+        full = lax.dynamic_update_slice_in_dim(full, part, (here ^ mask) * height, axis=join)
+    return full
 
 
 def build_tiles(weights_group, exchange_group, basis):
@@ -94,12 +110,11 @@
     )
     built_tiles = built_tiles.reshape(row_devs, col_devs, CAP, spline_count, spline_count)
     received, idents = (
-        lax.all_to_all(
+        pairwise_exchange(
             lax.all_to_all(built_tiles, "prow", split_axis=0, concat_axis=0, tiled=True),
             "pcol",
-            split_axis=1,
-            concat_axis=1,
-            tiled=True,
+            1,
+            1,
         ),
         lax.all_to_all(
             lax.all_to_all(

time: 1380 us -> 1250 us (0.906)
  waiting for transfers between devices: 982 us -> 721 us
  blocking collectives: 21 us -> 153 us
    all_to_all x3 -> x0, waiting for transfers between devices: 619 us -> none  [the longest x1 619 us: on_device(): lax.all_to_all(lax.all_to_all(built_tiles, 'prow', split_axis=0, concat_a...]
    ppermute x0 -> x15, waiting for transfers between devices: none -> 357 us  [pairwise_exchange(): part = lax.ppermute(part, axis, [(d, d ^ mask) for d in range(ways)])]
    all_to_all x0 -> x2, blocking collectives: none -> 132 us  [the longest x1 124 us: on_device(): lax.all_to_all(lax.all_to_all(slot_ids.reshape(row_devs, col_devs, CAP),...]
    all_to_all x2 -> x0, local copies, waits for them, and re-layouts: 45.9 us -> none  [the longest x1 23 us: on_device(): lax.all_to_all(built_tiles, 'prow', split_axis=0, concat_axis=0, tiled=True)]
    reshape x0 -> x1, local copies, waits for them, and re-layouts: none -> 43.9 us  [on_device(): built_tiles.reshape(row_devs, col_devs, CAP, spline_count, spline_count)]
    dynamic_update_slice x32 -> x15, local copies, waits for them, and re-layouts: 69.1 us -> 31.3 us  [pairwise_exchange(): lax.dynamic_update_slice_in_dim(full, part, (here ^ mask) * height, axis=...]
    ppermute x0 -> x15, starting transfers between devices: none -> 30.7 us  [pairwise_exchange(): part = lax.ppermute(part, axis, [(d, d ^ mask) for d in range(ways)])]
    all_to_all x3 -> x0, starting transfers between devices: 19.8 us -> none  [the longest x1 8.27 us: on_device(): lax.all_to_all(lax.all_to_all(slot_ids.reshape(row_devs, col_devs, CAP),...]
  transfers between devices with their start and end apart: 4 -> 16, of which waited for: 2 -> 10; matrix products, arithmetic and copies ran while one was open for 16% -> 2% of each run, Pallas kernels for 0% -> 0%
where the time goes in v1:
time: 1250 us; the launch traced here: 1240 us
  waiting for transfers between devices  721 us (58%)
  local copies, waits for them, and re-layouts  224 us (18%)
  blocking collectives  153 us (12%)
  matrix products  107 us (9%)
  starting transfers between devices  37.8 us (3%)
    all_to_all x1, waiting for transfers between devices, on_device(): lax.all_to_all(built_tiles, 'prow', split_axis=0, concat_axis=0, tiled=True)  364 us
    ppermute x15, waiting for transfers between devices, pairwise_exchange(): part = lax.ppermute(part, axis, [(d, d ^ mask) for d in range(ways)])  357 us
    all_to_all x1, blocking collectives, on_device(): lax.all_to_all(lax.all_to_all(slot_ids.reshape(row_devs, col_devs, CAP),...  124 us
    unnamed x44, local copies, waits for them, and re-layouts  60.7 us
    dot_general x16, matrix products, build_tiles(): jnp.einsum('qa,gqb->gab', inner_rows, exchange_group, preferred_element_t...  53.3 us
    dot_general x1, local copies, waits for them, and re-layouts, sum_blocks(): jnp.dot(select, built_tiles.reshape(built_tiles.shape[0], spline_width *...  43.9 us
    reshape x1, local copies, waits for them, and re-layouts, on_device(): built_tiles.reshape(row_devs, col_devs, CAP, spline_count, spline_count)  43.9 us
    dynamic_update_slice x15, local copies, waits for them, and re-layouts, pairwise_exchange(): lax.dynamic_update_slice_in_dim(full, part, (here ^ mask) * height, axis=...  31.3 us
  transfers between devices with their start and end apart: 16, of which 10 were waited for; matrix products, arithmetic and copies ran while one was open for 2% of the time, Pallas kernels for 0%

profile of v1, /device:TPU:80, one launch (start us, length us, event | category | flops | bytes accessed | tf_op | source)
XLA Modules:
  0.0 1242.9 jit_solution(8863728128588895684)
XLA Ops:
  1.6 21.0 %all-gather = bf16[16,4,512]{2,1,0:T(4,128)(2,1)S(1)} all-gather(bf16[1,4,512]{2,1,0:T(4,128)(2,1)} %bitcast.71), channel_id=1, replica_groups=mesh['prow'=8,'pcol'=16] {'pcol'}, dimensions={0}, use_global_device_ids=true | all-gather | bytes 69632 | tf_op jit(solution)/shard_map/all_gather | solution.py:54
  22.6 13.9 %copy.38 = bf16[24,8,128,256]{3,1,2,0:T(8,128)(2,1)} copy(bf16[24,8,128,256]{3,2,1,0:T(8,128)(2,1)} %bitcast.62) | data formatting | bytes 25165824
  38.2 12.8 %convolution_convert_fusion = bf16[256,32768]{1,0:T(8,128)(2,1)} fusion(bf16[192,32768]{1,0:T(8,128)(2,1)} %bitcast.59, s32[192]{0:T(256)S(1)} %copy-done.18), kind=kOutput, calls=%fused_computation.13 | convolution fusion | flops 3229663232 | bytes 29360896 | tf_op jit(solution)/shard_map/dot_general | solution.py:97
  51.0 15.7 %copy.39 = bf16[32,8,128,256]{3,2,1,0:T(8,128)(2,1)} copy(bf16[32,8,128,256]{3,1,2,0:T(8,128)(2,1)} %bitcast.58) | data formatting | bytes 33554432
  66.7 76.1 %while.10 = (s32[]{:T(128)}, bf16[16,16,256,256]{2,3,1,0:T(8,128)(2,1)}, bf16[16,16,512]{2,1,0:T(8,128)(2,1)S(1)}, bf16[512,256]{1,0:T(8,128)(2,1)S(1)}, bf16[16,16,128,256]{3,2,1,0:T(8,128)(2,1)}, /*index=5*/s32[]{:T(128)}) while((s32[]{:T(128)}, bf16[16,16,256,256]{2,3,1,0:T(8,128)(2,1)}, bf16[16,16,512]{2,1,0:T(8,128)(2,1)S(1)}, ...), condition=%wide.region_4.5_spmd, body=%wide.region_3.4_spmd.sunk | while | flops 1348476928 | bytes 13288529 | solution.py:104
  68.1 3.3 bitcast_dynamic-update-slice_fusion.2
  72.8 3.3 bitcast_dynamic-update-slice_fusion.2
  77.6 3.4 bitcast_dynamic-update-slice_fusion.2
  82.4 3.4 bitcast_dynamic-update-slice_fusion.2
  87.2 3.3 bitcast_dynamic-update-slice_fusion.2
  91.9 3.3 bitcast_dynamic-update-slice_fusion.2
  96.7 3.3 bitcast_dynamic-update-slice_fusion.2
  101.4 3.3 bitcast_dynamic-update-slice_fusion.2
  106.1 3.3 bitcast_dynamic-update-slice_fusion.2
  110.9 3.3 bitcast_dynamic-update-slice_fusion.2
  115.6 3.4 bitcast_dynamic-update-slice_fusion.2
  120.4 3.4 bitcast_dynamic-update-slice_fusion.2
  125.2 3.3 bitcast_dynamic-update-slice_fusion.2
  130.0 3.3 bitcast_dynamic-update-slice_fusion.2
  134.7 3.3 bitcast_dynamic-update-slice_fusion.2
  139.5 3.3 bitcast_dynamic-update-slice_fusion.2
  142.8 43.9 %copy.32 = bf16[8,16,2,256,256]{4,3,2,1,0:T(8,128)(2,1)} copy(bf16[8,16,2,256,256]{3,4,2,1,0:T(8,128)(2,1)} %bitcast.60) | data formatting | bytes 67108864 | tf_op jit(solution)/shard_map/reshape | solution.py:111
  186.6 7.1 all-to-all-start.2
  193.8 364.2 %all-to-all-done.2 = bf16[8,16,2,256,256]{4,3,2,1,0:T(8,128)(2,1)} async-done(((bf16[8,16,2,256,256]{4,3,2,1,0:T(8,128)(2,1)}), bf16[8,16,2,256,256]{4,3,2,1,0:T(8,128)(2,1)}, u32[]{:S(2)}, u32[]{:S(2)}) %all-to-all-start.2) | async-done | bytes 33554464 | tf_op jit(solution)/shard_map/all_to_all | solution.py:114
  558.0 10.9 broadcast_in_dim.55
  568.9 16.9 %constant_dynamic-slice_fusion.14 = (bf16[8,1,2,256,256]{4,3,2,1,0:T(8,128)(2,1)S(1)}, bf16[8,1,2,256,256]{4,3,2,1,0:T(8,128)(2,1)}, bf16[8,1,2,256,256]{4,3,2,1...) fusion(bf16[8,16,2,256,256]{4,3,2,1,0:T(8,128)(2,1)} %all-to-al, ...), kind=kLoop, calls=%fused_computation.68 | loop fusion | bytes 67108928 | tf_op jit(solution)/shard_map/dynamic_slice | solution.py:20
  585.8 3.6 collective-permute-start.9
  589.4 2.8 collective-permute-start.8
  592.3 2.1 collective-permute-start.7
  594.3 1.4 collective-permute-start.6
  595.8 1.6 collective-permute-start.5
  597.4 40.9 %collective-permute-done.9 = bf16[8,1,2,256,256]{4,3,2,1,0:T(8,128)(2,1)S(1)} collective-permute-done((bf16[8,1,2,256,256]{4,3,2,1,0:T(8,128)(2,1)S(1)}, bf16[8,1,2,256,256]{4,3,2,1,0:T(8,128)(2,1)S(1)}, u32[]{:S(2)}, u32[]{:S(2)}) %collective-permute-start.9) | collective-permute-done | bytes 2097184 | tf_op jit(solution)/shard_map/ppermute | solution.py:22
  638.3 2.7 collective-permute-start.4
  641.0 42.7 %collective-permute-done.8 = bf16[8,1,2,256,256]{4,3,2,1,0:T(8,128)(2,1)S(1)} collective-permute-done((bf16[8,1,2,256,256]{4,3,2,1,0:T(8,128)(2,1)S(1)}, bf16[8,1,2,256,256]{4,3,2,1,0:T(8,128)(2,1)S(1)}, u32[]{:S(2)}, u32[]{:S(2)}) %collective-permute-start.8) | collective-permute-done | bytes 2097184 | tf_op jit(solution)/shard_map/ppermute | solution.py:22
  684.5 42.8 %collective-permute-done.7 = bf16[8,1,2,256,256]{4,3,2,1,0:T(8,128)(2,1)S(1)} collective-permute-done((bf16[8,1,2,256,256]{4,3,2,1,0:T(8,128)(2,1)S(1)}, bf16[8,1,2,256,256]{4,3,2,1,0:T(8,128)(2,1)S(1)}, u32[]{:S(2)}, u32[]{:S(2)}) %collective-permute-start.7) | collective-permute-done | bytes 2097184 | tf_op jit(solution)/shard_map/ppermute | solution.py:22
  727.3 1.9 collective-permute-start.2
  729.2 43.2 %collective-permute-done.6 = bf16[8,1,2,256,256]{4,3,2,1,0:T(8,128)(2,1)S(1)} collective-permute-done((bf16[8,1,2,256,256]{4,3,2,1,0:T(8,128)(2,1)S(1)}, bf16[8,1,2,256,256]{4,3,2,1,0:T(8,128)(2,1)S(1)}, u32[]{:S(2)}, u32[]{:S(2)}) %collective-permute-start.6) | collective-permute-done | bytes 2097184 | tf_op jit(solution)/shard_map/ppermute | solution.py:22
  772.4 2.9 collective-permute-start
  775.2 43.4 %collective-permute-done.5 = bf16[8,1,2,256,256]{4,3,2,1,0:T(8,128)(2,1)S(1)} collective-permute-done((bf16[8,1,2,256,256]{4,3,2,1,0:T(8,128)(2,1)S(1)}, bf16[8,1,2,256,256]{4,3,2,1,0:T(8,128)(2,1)S(1)}, u32[]{:S(2)}, u32[]{:S(2)}) %collective-permute-start.5) | collective-permute-done | bytes 2097184 | tf_op jit(solution)/shard_map/ppermute | solution.py:22
  818.7 2.1 collective-permute-start.1
  820.7 41.8 %collective-permute-done.4 = bf16[8,1,2,256,256]{4,3,2,1,0:T(8,128)(2,1)S(1)} collective-permute-done((bf16[8,1,2,256,256]{4,3,2,1,0:T(8,128)(2,1)S(1)}, bf16[8,1,2,256,256]{4,3,2,1,0:T(8,128)(2,1)S(1)}, u32[]{:S(2)}, u32[]{:S(2)}) %collective-permute-start.4) | collective-permute-done | bytes 2097184 | tf_op jit(solution)/shard_map/ppermute | solution.py:22
  862.5 2.5 collective-permute-start.10
  865.0 42.5 %collective-permute-done.3 = bf16[8,1,2,256,256]{4,3,2,1,0:T(8,128)(2,1)S(1)} collective-permute-done((bf16[8,1,2,256,256]{4,3,2,1,0:T(8,128)(2,1)S(1)}, bf16[8,1,2,256,256]{4,3,2,1,0:T(8,128)(2,1)S(1)}, u32[]{:S(2)}, u32[]{:S(2)}) %collective-permute-start.3) | collective-permute-done | bytes 2097184 | tf_op jit(solution)/shard_map/ppermute | solution.py:22
  908.3 1.5 collective-permute-start.12
  910.2 7.7 all_to_all.15
  917.9 124.1 %all_to_all.16 = s32[8,16,2]{0,2,1:T(2,128)S(1)} all-to-all(s32[8,16,2]{0,2,1:T(2,128)S(1)} %copy.29), channel_id=1, replica_groups=mesh['prow'=8,'pcol'=16] {'pcol'}, dimensions={1} | all-to-all | bytes 2048 | tf_op jit(solution)/shard_map/all_to_all | solution.py:119
  1042.4 2.8 collective-permute-start.13
  1045.2 3.2 constant_dynamic-update-slice_fusion.13
  1048.4 1.5 collective-permute-start.14
  1049.8 3.1 constant_dynamic-update-slice_fusion.12
  1052.9 3.2 constant_dynamic-update-slice_fusion.11
  1056.1 1.4 constant_dynamic-update-slice_fusion.10
  1057.6 1.4 constant_dynamic-update-slice_fusion.9
  1059.0 1.4 constant_dynamic-update-slice_fusion.8
  1063.2 1.4 constant_dynamic-update-slice_fusion.5
  1066.0 3.0 constant_dynamic-update-slice_fusion.3
  1069.1 3.0 constant_dynamic-update-slice_fusion.2
  1072.1 3.1 constant_dynamic-update-slice_fusion.1
  1075.2 18.9 %collective-permute-done.13 = bf16[8,1,2,256,256]{4,3,2,1,0:T(8,128)(2,1)S(1)} collective-permute-done((bf16[8,1,2,256,256]{4,3,2,1,0:T(8,128)(2,1)}, bf16[8,1,2,256,256]{4,3,2,1,0:T(8,128)(2,1)S(1)}, u32[]{:S(2)}, u32[]{:S(2)}) %collective-permute-start.13) | collective-permute-done | bytes 2097184 | tf_op jit(solution)/shard_map/ppermute | solution.py:22
  1095.4 40.6 %collective-permute-done.14 = bf16[8,1,2,256,256]{4,3,2,1,0:T(8,128)(2,1)S(1)} collective-permute-done((bf16[8,1,2,256,256]{4,3,2,1,0:T(8,128)(2,1)S(1)}, bf16[8,1,2,256,256]{4,3,2,1,0:T(8,128)(2,1)S(1)}, u32[]{:S(2)}, u32[]{:S(2)}) %collective-permute-start.14) | collective-permute-done | bytes 2097184 | tf_op jit(solution)/shard_map/ppermute | solution.py:22
  1137.4 31.0 %copy.40 = bf16[32,8,256,256]{3,1,2,0:T(8,128)(2,1)} copy(bf16[32,8,256,256]{3,2,1,0:T(8,128)(2,1)} %bitcast.55) | data formatting | bytes 67108864
  1168.4 43.9 %copy.35 = bf16[65536,256]{1,0:T(8,128)(2,1)} copy(bf16[65536,256]{0,1:T(8,128)(2,1)} %bitcast.57) | data formatting | bytes 67108864 | tf_op jit(solution)/shard_map/dot_general | solution.py:45
  1212.4 19.0 %convolution_convert_fusion.1 = bf16[64,256,256]{2,0,1:T(8,128)(2,1)} fusion(bf16[256,256,256]{2,1,0:T(8,128)(2,1)} %bitcast.56, s32[256]{0:T(256)S(1)} %eq.101), kind=kOutput, calls=%fused_computation.14 | convolution fusion | flops 2151694336 | bytes 41944064 | tf_op jit(solution)/shard_map/dot_general | solution.py:45
  1231.3 11.5 copy.36
  (133 shorter events, 34.9 us)
Async XLA Ops:
  0.0 37.3 %copy-start = (f32[8,512]{1,0:T(8,128)S(1)}, f32[8,512]{1,0:T(8,128)}, u32[]{:S(2)}) copy-start(f32[8,512]{1,0:T(8,128)} %param.11) | copy-start | bytes 49156
  22.6 14.0 %copy-start.19 = (s32[256]{0:T(256)S(1)}, s32[256]{0:T(256)}, u32[]{:S(2)}) copy-start(s32[256]{0:T(256)} %param.13) | copy-start | bytes 3076
  22.6 15.1 %copy-start.18 = (s32[192]{0:T(256)S(1)}, s32[192]{0:T(256)}, u32[]{:S(2)}) copy-start(s32[192]{0:T(256)} %param.15) | copy-start | bytes 2308
  51.0 15.7 %copy-start.2 = (bf16[512,256]{1,0:T(8,128)(2,1)S(1)}, bf16[512,256]{1,0:T(8,128)(2,1)}, u32[]{:S(2)}) copy-start(bf16[512,256]{1,0:T(8,128)(2,1)} %param.10) | copy-start | bytes 786436
  186.6 371.4 %all-to-all-start.2 = ((bf16[8,16,2,256,256]{4,3,2,1,0:T(8,128)(2,1)}), bf16[8,16,2,256,256]{4,3,2,1,0:T(8,128)(2,1)}, u32[]{:S(2)}, u32[]{:S(2)}) async-start(bf16[8,16,2,256,256]{4,3,2,1,0:T(8,128)(2,1)} %copy.32), calls=%async_computation.2 | async-start | bytes 67108864 | tf_op jit(solution)/shard_map/all_to_all | solution.py:114
  585.8 52.5 %collective-permute-start.9 = (bf16[8,1,2,256,256]{4,3,2,1,0:T(8,128)(2,1)S(1)}, bf16[8,1,2,256,256]{4,3,2,1,0:T(8,128)(2,1)S(1)}, u32[]{:S(2)}, u32[]{:S(2)}) collective-permute-start(bf16[8,1,2,256,256]{4,3,2,1,0:T(8,128)(2,1)S(1)} %get-tuple-element.70), channel_id=1, source_target_pairs={{0,10},{1,11},{2,8},{3,9},{4,14},{5,15},{6,12},{7,13},{8,2},{9,3},... | collective-permute-start | bytes 6291464 | tf_op jit(solution)/shard_map/ppermute | solution.py:22
  589.4 94.3 %collective-permute-start.8 = (bf16[8,1,2,256,256]{4,3,2,1,0:T(8,128)(2,1)S(1)}, bf16[8,1,2,256,256]{4,3,2,1,0:T(8,128)(2,1)S(1)}, u32[]{:S(2)}, u32[]{:S(2)}) collective-permute-start(bf16[8,1,2,256,256]{4,3,2,1,0:T(8,128)(2,1)S(1)} %get-tuple-element.71), channel_id=1, source_target_pairs={{0,9},{1,8},{2,11},{3,10},{4,13},{5,12},{6,15},{7,14},{8,1},{9,0},... | collective-permute-start | bytes 6291464 | tf_op jit(solution)/shard_map/ppermute | solution.py:22
  592.3 135.1 %collective-permute-start.7 = (bf16[8,1,2,256,256]{4,3,2,1,0:T(8,128)(2,1)S(1)}, bf16[8,1,2,256,256]{4,3,2,1,0:T(8,128)(2,1)S(1)}, u32[]{:S(2)}, u32[]{:S(2)}) collective-permute-start(bf16[8,1,2,256,256]{4,3,2,1,0:T(8,128)(2,1)S(1)} %get-tuple-element.72), channel_id=1, source_target_pairs={{0,8},{1,9},{2,10},{3,11},{4,12},{5,13},{6,14},{7,15},{8,0},{9,1},... | collective-permute-start | bytes 6291464 | tf_op jit(solution)/shard_map/ppermute | solution.py:22
  594.3 178.0 %collective-permute-start.6 = (bf16[8,1,2,256,256]{4,3,2,1,0:T(8,128)(2,1)S(1)}, bf16[8,1,2,256,256]{4,3,2,1,0:T(8,128)(2,1)S(1)}, u32[]{:S(2)}, u32[]{:S(2)}) collective-permute-start(bf16[8,1,2,256,256]{4,3,2,1,0:T(8,128)(2,1)S(1)} %get-tuple-element.73), channel_id=1, source_target_pairs={{0,7},{1,6},{2,5},{3,4},{4,3},{5,2},{6,1},{7,0},{8,15},{9,14},{10,... | collective-permute-start | bytes 6291464 | tf_op jit(solution)/shard_map/ppermute | solution.py:22
  595.8 222.9 %collective-permute-start.5 = (bf16[8,1,2,256,256]{4,3,2,1,0:T(8,128)(2,1)S(1)}, bf16[8,1,2,256,256]{4,3,2,1,0:T(8,128)(2,1)S(1)}, u32[]{:S(2)}, u32[]{:S(2)}) collective-permute-start(bf16[8,1,2,256,256]{4,3,2,1,0:T(8,128)(2,1)S(1)} %get-tuple-element.74), channel_id=1, source_target_pairs={{0,6},{1,7},{2,4},{3,5},{4,2},{5,3},{6,0},{7,1},{8,14},{9,15},{10,... | collective-permute-start | bytes 6291464 | tf_op jit(solution)/shard_map/ppermute | solution.py:22
  638.3 269.9 %copy-start.3 = (bf16[8,1,2,256,256]{4,3,2,1,0:T(8,128)(2,1)}, bf16[8,1,2,256,256]{4,3,2,1,0:T(8,128)(2,1)S(1)}, u32[]{:S(2)}) copy-start(bf16[8,1,2,256,256]{4,3,2,1,0:T(8,128)(2,1)S(1)} %collective-permute-done.9) | copy-start | bytes 6291460
  638.3 224.2 %collective-permute-start.4 = (bf16[8,1,2,256,256]{4,3,2,1,0:T(8,128)(2,1)S(1)}, bf16[8,1,2,256,256]{4,3,2,1,0:T(8,128)(2,1)S(1)}, u32[]{:S(2)}, u32[]{:S(2)}) collective-permute-start(bf16[8,1,2,256,256]{4,3,2,1,0:T(8,128)(2,1)S(1)} %get-tuple-element.75), channel_id=1, source_target_pairs={{0,5},{1,4},{2,7},{3,6},{4,1},{5,0},{6,3},{7,2},{8,13},{9,12},{10,... | collective-permute-start | bytes 6291464 | tf_op jit(solution)/shard_map/ppermute | solution.py:22
  683.7 223.9 %copy-start.5 = (bf16[8,1,2,256,256]{4,3,2,1,0:T(8,128)(2,1)}, bf16[8,1,2,256,256]{4,3,2,1,0:T(8,128)(2,1)S(1)}, u32[]{:S(2)}) copy-start(bf16[8,1,2,256,256]{4,3,2,1,0:T(8,128)(2,1)S(1)} %collective-permute-done.8) | copy-start | bytes 6291460
  683.7 223.8 %collective-permute-start.3 = (bf16[8,1,2,256,256]{4,3,2,1,0:T(8,128)(2,1)S(1)}, bf16[8,1,2,256,256]{4,3,2,1,0:T(8,128)(2,1)S(1)}, u32[]{:S(2)}, u32[]{:S(2)}) collective-permute-start(bf16[8,1,2,256,256]{4,3,2,1,0:T(8,128)(2,1)S(1)} %get-tuple-element.76), channel_id=1, source_target_pairs={{0,4},{1,5},{2,6},{3,7},{4,0},{5,1},{6,2},{7,3},{8,12},{9,13},{10,... | collective-permute-start | bytes 6291464 | tf_op jit(solution)/shard_map/ppermute | solution.py:22
  727.3 180.3 %copy-start.7 = (bf16[8,1,2,256,256]{4,3,2,1,0:T(8,128)(2,1)}, bf16[8,1,2,256,256]{4,3,2,1,0:T(8,128)(2,1)S(1)}, u32[]{:S(2)}) copy-start(bf16[8,1,2,256,256]{4,3,2,1,0:T(8,128)(2,1)S(1)} %collective-permute-done.7) | copy-start | bytes 6291460
  727.3 180.9 %collective-permute-start.2 = (bf16[8,1,2,256,256]{4,3,2,1,0:T(8,128)(2,1)S(1)}, bf16[8,1,2,256,256]{4,3,2,1,0:T(8,128)(2,1)S(1)}, u32[]{:S(2)}, u32[]{:S(2)}) collective-permute-start(bf16[8,1,2,256,256]{4,3,2,1,0:T(8,128)(2,1)S(1)} %get-tuple-element.77), channel_id=1, source_target_pairs={{0,3},{1,2},{2,1},{3,0},{4,7},{5,6},{6,5},{7,4},{8,11},{9,10},{10,... | collective-permute-start | bytes 6291464 | tf_op jit(solution)/shard_map/ppermute | solution.py:22
  772.4 135.2 %copy-start.9 = (bf16[8,1,2,256,256]{4,3,2,1,0:T(8,128)(2,1)}, bf16[8,1,2,256,256]{4,3,2,1,0:T(8,128)(2,1)S(1)}, u32[]{:S(2)}) copy-start(bf16[8,1,2,256,256]{4,3,2,1,0:T(8,128)(2,1)S(1)} %collective-permute-done.6) | copy-start | bytes 6291460
  772.4 270.0 %collective-permute-start = (bf16[8,1,2,256,256]{4,3,2,1,0:T(8,128)(2,1)}, bf16[8,1,2,256,256]{4,3,2,1,0:T(8,128)(2,1)}, u32[]{:S(2)}, u32[]{:S(2)}) collective-permute-start(bf16[8,1,2,256,256]{4,3,2,1,0:T(8,128)(2,1)} %get-tuple-element.79), channel_id=1, source_target_pairs={{0,1},{1,0},{2,3},{3,2},{4,5},{5,4},{6,7},{7,6},{8,9},{9,8},{10,11... | collective-permute-start | bytes 6291464 | tf_op jit(solution)/shard_map/ppermute | solution.py:22
  818.7 88.9 %copy-start.11 = (bf16[8,1,2,256,256]{4,3,2,1,0:T(8,128)(2,1)}, bf16[8,1,2,256,256]{4,3,2,1,0:T(8,128)(2,1)S(1)}, u32[]{:S(2)}) copy-start(bf16[8,1,2,256,256]{4,3,2,1,0:T(8,128)(2,1)S(1)} %collective-permute-done.5) | copy-start | bytes 6291460
  818.7 229.7 %collective-permute-start.1 = (bf16[8,1,2,256,256]{4,3,2,1,0:T(8,128)(2,1)}, bf16[8,1,2,256,256]{4,3,2,1,0:T(8,128)(2,1)}, u32[]{:S(2)}, u32[]{:S(2)}) collective-permute-start(bf16[8,1,2,256,256]{4,3,2,1,0:T(8,128)(2,1)} %get-tuple-element.78), channel_id=1, source_target_pairs={{0,2},{1,3},{2,0},{3,1},{4,6},{5,7},{6,4},{7,5},{8,10},{9,11},{10,... | collective-permute-start | bytes 6291464 | tf_op jit(solution)/shard_map/ppermute | solution.py:22
  862.5 45.7 %copy-start.13 = (bf16[8,1,2,256,256]{4,3,2,1,0:T(8,128)(2,1)}, bf16[8,1,2,256,256]{4,3,2,1,0:T(8,128)(2,1)S(1)}, u32[]{:S(2)}) copy-start(bf16[8,1,2,256,256]{4,3,2,1,0:T(8,128)(2,1)S(1)} %collective-permute-done.4) | copy-start | bytes 6291460
  862.5 203.5 %collective-permute-start.10 = (bf16[8,1,2,256,256]{4,3,2,1,0:T(8,128)(2,1)}, bf16[8,1,2,256,256]{4,3,2,1,0:T(8,128)(2,1)}, u32[]{:S(2)}, u32[]{:S(2)}) collective-permute-start(bf16[8,1,2,256,256]{4,3,2,1,0:T(8,128)(2,1)} %get-tuple-element.69), channel_id=1, source_target_pairs={{0,11},{1,10},{2,9},{3,8},{4,15},{5,14},{6,13},{7,12},{8,3},{9,2},... | collective-permute-start | bytes 6291464 | tf_op jit(solution)/shard_map/ppermute | solution.py:22
  907.6 2.2 copy-start.15
  907.6 161.5 %collective-permute-start.11 = (bf16[8,1,2,256,256]{4,3,2,1,0:T(8,128)(2,1)}, bf16[8,1,2,256,256]{4,3,2,1,0:T(8,128)(2,1)}, u32[]{:S(2)}, u32[]{:S(2)}) collective-permute-start(bf16[8,1,2,256,256]{4,3,2,1,0:T(8,128)(2,1)} %get-tuple-element.68), channel_id=1, source_target_pairs={{0,12},{1,13},{2,14},{3,15},{4,8},{5,9},{6,10},{7,11},{8,4},{9,5},... | collective-permute-start | bytes 6291464 | tf_op jit(solution)/shard_map/ppermute | solution.py:22
  908.2 1.5 copy-start.17
  908.3 163.9 %collective-permute-start.12 = (bf16[8,1,2,256,256]{4,3,2,1,0:T(8,128)(2,1)}, bf16[8,1,2,256,256]{4,3,2,1,0:T(8,128)(2,1)}, u32[]{:S(2)}, u32[]{:S(2)}) collective-permute-start(bf16[8,1,2,256,256]{4,3,2,1,0:T(8,128)(2,1)} %get-tuple-element.67), channel_id=1, source_target_pairs={{0,13},{1,12},{2,15},{3,14},{4,9},{5,8},{6,11},{7,10},{8,5},{9,4},... | collective-permute-start | bytes 6291464 | tf_op jit(solution)/shard_map/ppermute | solution.py:22
  1042.3 13.8 %copy-start.16 = (bf16[8,1,2,256,256]{4,3,2,1,0:T(8,128)(2,1)S(1)}, bf16[8,1,2,256,256]{4,3,2,1,0:T(8,128)(2,1)}, u32[]{:S(2)}) copy-start(bf16[8,1,2,256,256]{4,3,2,1,0:T(8,128)(2,1)} %copy-done.15) | copy-start | bytes 6291460
  1042.3 15.2 %copy-start.14 = (bf16[8,1,2,256,256]{4,3,2,1,0:T(8,128)(2,1)S(1)}, bf16[8,1,2,256,256]{4,3,2,1,0:T(8,128)(2,1)}, u32[]{:S(2)}) copy-start(bf16[8,1,2,256,256]{4,3,2,1,0:T(8,128)(2,1)} %copy-done.13) | copy-start | bytes 6291460
  1042.3 16.6 %copy-start.12 = (bf16[8,1,2,256,256]{4,3,2,1,0:T(8,128)(2,1)S(1)}, bf16[8,1,2,256,256]{4,3,2,1,0:T(8,128)(2,1)}, u32[]{:S(2)}) copy-start(bf16[8,1,2,256,256]{4,3,2,1,0:T(8,128)(2,1)} %copy-done.11) | copy-start | bytes 6291460
  1042.4 51.7 %collective-permute-start.13 = (bf16[8,1,2,256,256]{4,3,2,1,0:T(8,128)(2,1)}, bf16[8,1,2,256,256]{4,3,2,1,0:T(8,128)(2,1)S(1)}, u32[]{:S(2)}, u32[]{:S(2)}) collective-permute-start(bf16[8,1,2,256,256]{4,3,2,1,0:T(8,128)(2,1)} %get-tuple-element.66), channel_id=1, source_target_pairs={{0,14},{1,15},{2,12},{3,13},{4,10},{5,11},{6,8},{7,9},{8,6},{9,7},... | collective-permute-start | bytes 6291464 | tf_op jit(solution)/shard_map/ppermute | solution.py:22
  1045.2 15.2 %copy-start.10 = (bf16[8,1,2,256,256]{4,3,2,1,0:T(8,128)(2,1)S(1)}, bf16[8,1,2,256,256]{4,3,2,1,0:T(8,128)(2,1)}, u32[]{:S(2)}) copy-start(bf16[8,1,2,256,256]{4,3,2,1,0:T(8,128)(2,1)} %copy-done.9) | copy-start | bytes 6291460
  1048.4 13.5 %copy-start.8 = (bf16[8,1,2,256,256]{4,3,2,1,0:T(8,128)(2,1)S(1)}, bf16[8,1,2,256,256]{4,3,2,1,0:T(8,128)(2,1)}, u32[]{:S(2)}) copy-start(bf16[8,1,2,256,256]{4,3,2,1,0:T(8,128)(2,1)} %copy-done.7) | copy-start | bytes 6291460
  1048.4 87.7 %collective-permute-start.14 = (bf16[8,1,2,256,256]{4,3,2,1,0:T(8,128)(2,1)S(1)}, bf16[8,1,2,256,256]{4,3,2,1,0:T(8,128)(2,1)S(1)}, u32[]{:S(2)}, u32[]{:S(2)}) collective-permute-start(bf16[8,1,2,256,256]{4,3,2,1,0:T(8,128)(2,1)S(1)} %get-tuple-element.65), channel_id=1, source_target_pairs={{0,15},{1,14},{2,13},{3,12},{4,11},{5,10},{6,9},{7,8},{8,7},{9,6},... | collective-permute-start | bytes 6291464 | tf_op jit(solution)/shard_map/ppermute | solution.py:22
  1052.9 10.3 copy-start.6
  1056.1 8.5 copy-start.4
  1212.4 30.5 %copy-start.1 = (f32[8,512]{1,0:T(8,128)S(1)}, f32[8,512]{1,0:T(8,128)}, u32[]{:S(2)}) copy-start(f32[8,512]{1,0:T(8,128)} %param.11) | copy-start | bytes 49156
